TPU v7x, 256 devices: a whole 4x4x8 slice. The times are simulated.
256 devices in a mesh: row: 4 (over y), col: 16 (over z_hi, x, core), dep: 4 (over z_lo).
Axes of the slice: x: 4, y: 4, z: 8 (z_hi: 2, z_lo: 4; z = z_hi * 4 + z_lo), core: 2. Of those that a mesh axis runs over, the one named last changes fastest.
Arguments:
- grad_out: bfloat16 [4, 512, 12288], P('row', 'dep', 'col'), may hold values from -7 to 7
- out_weight: bfloat16 [8192, 12288], P('row', 'col'), may hold values from -0.09375 to 0.09375
- query_rows: bfloat16 [2048, 8192], P('dep', ('row', 'col')), may hold values from -6 to 6
- key_rows: bfloat16 [2048, 8192], P('dep', ('row', 'col')), may hold values from -6 to 6
- value_rows: bfloat16 [2048, 8192], P('dep', ('row', 'col')), may hold values from -7 to 7
- seg_lengths: int32 [8], replicated, may hold values from 1 to 1536, 2048 in all
Outputs:
- grad_weight: float32 [8192, 12288], P('row', 'col')
- grad_query: bfloat16 [2048, 8192], P('dep', ('row', 'col'))
- grad_key: bfloat16 [2048, 8192], P('dep', ('row', 'col'))
- grad_value: bfloat16 [2048, 8192], P('dep', ('row', 'col'))
All inputs are finite; a program needn't handle non-finite values.
Results may differ from a plain program's by a relative error of at most 0.029.
Values may be sent and summed in bfloat16 or wider, within the bound.
No kernel may reach another device: no remote copies, remote signals or barrier semaphores. Data moves between devices by JAX's collectives and lax.ppermute only.
A program may use at most 128 MiB of HBM per device.

v0:
```python
import math
import jax
import jax.numpy as jnp
from jax import lax
from jax.sharding import Mesh
from jax.sharding import PartitionSpec as P

NEG_FILL = -1e30
FAR = 1 << 30
COL = ("zh", "x", "core")
DEP = "zl"


def segment_count(positions, seg_ends):
    return jnp.sum((positions[:, None] >= seg_ends[None, :]).astype(jnp.int32), axis=1)


def shift(x, axis, n, s):
    return lax.ppermute(x, axis, [(i, (i + s) % n) for i in range(n)])


def shift_open(x, axis, n, s):
    return lax.ppermute(x, axis, [(i, i + s) for i in range(n) if 0 <= i + s < n])


def roll_rows(x, amount, axis):
    size = x.shape[axis]
    doubled = jnp.concatenate([x, x], axis=axis)
    return lax.dynamic_slice_in_dim(doubled, (size - amount) % size, size, axis=axis)


def rolled_gather(x, axis, n, stack_axis=0):
    parts = [x] + [shift(x, axis, n, -s) for s in range(1, n)]
    return jnp.stack(parts, axis=stack_axis)


def pp_reduce_scatter(x, axis, n, dim):
    me = lax.axis_index(axis)
    acc = lax.dynamic_index_in_dim(x, me, dim, keepdims=False).astype(jnp.float32)
    for s in range(1, n):
        send = lax.dynamic_index_in_dim(x, (me + s) % n, dim, keepdims=False)
        acc = acc + shift(send, axis, n, s).astype(jnp.float32)
    return acc


def pp_reduce_scatter_cols(x, axis, n):
    me = lax.axis_index(axis)
    width = x.shape[1] // n
    acc = lax.dynamic_slice_in_dim(x, me * width, width, axis=1).astype(jnp.float32)
    for s in range(1, n):
        send = lax.dynamic_slice_in_dim(x, (me + s) % n * width, width, axis=1)
        acc = acc + shift(send, axis, n, s).astype(jnp.float32)
    return acc


def make_shards(n_zh, n_x, n_core, n_row, n_dep):

    def shards(grad_out, out_weight, query_rows, key_rows, value_rows, seg_lengths):
        n_tok, feat = (grad_out.shape[1], grad_out.shape[2])
        tok_depth = n_row * n_tok
        head_dim = query_rows.shape[1]
        inv_root = 1.0 / math.sqrt(head_dim)
        me_r = lax.axis_index("row")
        me_d = lax.axis_index(DEP)
        local = grad_out[0]
        grad_rows = rolled_gather(local, "row", n_row).reshape(tok_depth, feat)
        kv = jnp.concatenate([key_rows, value_rows], axis=1)
        kv_all = jnp.stack(
            [kv] + [shift_open(kv, DEP, n_dep, t) for t in range(1, n_dep)], axis=0
        ).reshape(n_dep * tok_depth, 2 * head_dim)
        keys_all, values_all = (kv_all[:, :head_dim], kv_all[:, head_dim:])
        by_depth = rolled_gather(local, DEP, n_dep)
        src_depth = me_d - jnp.arange(n_dep, dtype=jnp.int32)
        key_pos = (
            jnp.where(src_depth >= 0, src_depth * tok_depth, FAR)[:, None]
            + jnp.arange(tok_depth, dtype=jnp.int32)[None, :]
        ).reshape(-1)
        seg_ends = jnp.cumsum(seg_lengths)
        key_seg = segment_count(key_pos, seg_ends)
        query_rows = roll_rows(query_rows, -me_r * n_tok, 0)
        query_pos = (
            me_d * tok_depth + (jnp.arange(tok_depth, dtype=jnp.int32) + me_r * n_tok) % tok_depth
        )
        query_seg = segment_count(query_pos, seg_ends)
        allowed = (query_seg[:, None] == key_seg[None, :]) & (
            key_pos[None, :] <= query_pos[:, None]
        )
        scores = (
            jnp.einsum("qh,kh->qk", query_rows, keys_all, preferred_element_type=jnp.float32)
            * inv_root
        )
        masked = jnp.where(allowed, scores, NEG_FILL)
        row_max = jnp.max(masked, axis=1, keepdims=True)
        exponent = jnp.where(allowed, jnp.exp(masked - row_max), 0.0)
        row_sum = jnp.sum(exponent, axis=1, keepdims=True)
        prob_full = exponent * (1.0 / row_sum)
        prob_half = prob_full.astype(jnp.bfloat16)
        context = jnp.dot(prob_half, values_all, preferred_element_type=jnp.float32).astype(
            jnp.bfloat16
        )
        weight_perm = jnp.transpose(
            out_weight.reshape(n_zh, n_x, n_core, head_dim, feat), (2, 1, 0, 3, 4)
        ).reshape(-1, feat)
        partial = jnp.einsum(
            "tf,hf->th", grad_rows, weight_perm, preferred_element_type=jnp.float32
        ).astype(jnp.bfloat16)
        partial = pp_reduce_scatter_cols(partial, "core", n_core).astype(jnp.bfloat16)
        context, partial, by_depth = lax.optimization_barrier((context, partial, by_depth))
        by_depth = roll_rows(by_depth, me_d, 0)
        rows_all = rolled_gather(by_depth, "row", n_row, stack_axis=1)
        ctx_all = lax.all_gather(context[None], ("zh", DEP, "x", "core"), axis=0, tiled=True)
        ctx_all = ctx_all.reshape(n_zh, n_dep, n_x, n_core, tok_depth, head_dim)
        partial = pp_reduce_scatter_cols(partial, "x", n_x).astype(jnp.bfloat16)
        partial = pp_reduce_scatter_cols(partial, "zh", n_zh).astype(jnp.bfloat16)
        context_grad = partial
        grad_prob = jnp.dot(context_grad, values_all.T, preferred_element_type=jnp.float32)
        delta_row = jnp.sum(prob_full * grad_prob, axis=1, keepdims=True)
        grad_score = (prob_full * (grad_prob - delta_row)).astype(jnp.bfloat16)
        grad_query = (
            jnp.dot(grad_score, keys_all, preferred_element_type=jnp.float32) * inv_root
        ).astype(jnp.bfloat16)
        key_partial = (
            jnp.einsum("qk,qh->kh", grad_score, query_rows, preferred_element_type=jnp.float32)
            * inv_root
        ).astype(jnp.bfloat16)
        value_partial = jnp.einsum(
            "qk,qh->kh", prob_half, context_grad, preferred_element_type=jnp.float32
        ).astype(jnp.bfloat16)
        kv_partial = jnp.concatenate([key_partial, value_partial], axis=1).reshape(
            n_dep, tok_depth, 2 * head_dim
        )
        kv_grad = kv_partial[0].astype(jnp.float32)
        for s in range(1, n_dep):
            kv_grad = kv_grad + shift_open(kv_partial[s], DEP, n_dep, -s).astype(jnp.float32)
        kv_grad = kv_grad.astype(jnp.bfloat16)
        grad_key, grad_value = (kv_grad[:, :head_dim], kv_grad[:, head_dim:])
        grad_weight = None
        for depth in range(n_dep):
            piece = jnp.einsum(
                "zxcth,tf->zxchf",
                ctx_all[:, depth],
                rows_all[depth].reshape(tok_depth, feat),
                preferred_element_type=jnp.float32,
            )
            grad_weight = piece if grad_weight is None else grad_weight + piece
            if depth < n_dep - 1:
                grad_weight = lax.optimization_barrier(grad_weight)
        grad_weight = grad_weight.reshape(n_zh * n_x * n_core * head_dim, feat)
        grad_query = roll_rows(grad_query, me_r * n_tok, 0)
        return (grad_weight, grad_query, grad_key, grad_value)

    return shards


def solution(mesh):
    n_row, n_col, n_dep = (mesh.shape["row"], mesh.shape["col"], mesh.shape["dep"])
    n_zh, n_core = (2, 2)
    n_x = n_col // (n_zh * n_core)
    fine = Mesh(mesh.devices.reshape(n_row, n_zh, n_x, n_core, n_dep), ("row",) + COL + (DEP,))
    in_specs = (
        P("row", DEP, COL),
        P("row", COL),
        P(DEP, ("row",) + COL),
        P(DEP, ("row",) + COL),
        P(DEP, ("row",) + COL),
        P(),
    )
    out_specs = (
        P("row", COL),
        P(DEP, ("row",) + COL),
        P(DEP, ("row",) + COL),
        P(DEP, ("row",) + COL),
    )
    return jax.shard_map(
        make_shards(n_zh, n_x, n_core, n_row, n_dep),
        mesh=fine,
        in_specs=in_specs,
        out_specs=out_specs,
        check_vma=False,
    )
```

profile of v0, /device:TPU:1, one launch (start us, length us, event | category | flops | bytes accessed | tf_op | source)
XLA Modules:
  0.0 173.1 jit_solution(16478914064638914497)
XLA Ops:
  7.2 2.5 %collective-permute-start.9 = (bf16[128,768]{1,0:T(8,128)(2,1)}, bf16[128,768]{1,0:T(8,128)(2,1)S(1)}, u32[]{:S(2)}, u32[]{:S(2)}) collective-permute-start(bf16[128,768]{1,0:T(8,128)(2,1)} %bitcast.94), channel_id=1, source_target_pairs={{0,1},{1,2},{2,3},{3,0},{4,5},{5,6},{6,7},{7,4},{8,9},{9,10},{10,1... | collective-permute-start | bytes 589832 | tf_op jit(solution)/shard_map/ppermute | solution.py:19
  9.8 3.0 %collective-permute-start.8 = (bf16[128,768]{1,0:T(8,128)(2,1)}, bf16[128,768]{1,0:T(8,128)(2,1)S(1)}, u32[]{:S(2)}, u32[]{:S(2)}) collective-permute-start(bf16[128,768]{1,0:T(8,128)(2,1)} %bitcast.95), channel_id=1, source_target_pairs={{0,2},{1,3},{2,0},{3,1},{4,6},{5,7},{6,4},{7,5},{8,10},{9,11},{10,... | collective-permute-start | bytes 589832 | tf_op jit(solution)/shard_map/ppermute | solution.py:19
  12.8 0.7 collective-permute-start.7
  13.5 1.3 collective-permute-start.5
  14.8 2.6 %collective-permute-start.4 = (bf16[128,768]{1,0:T(8,128)(2,1)}, bf16[128,768]{1,0:T(8,128)(2,1)S(1)}, u32[]{:S(2)}, u32[]{:S(2)}) collective-permute-start(bf16[128,768]{1,0:T(8,128)(2,1)} %bitcast.98), channel_id=1, source_target_pairs={{0,128},{64,192},{128,0},{192,64},{1,129},{65,193},{129,1},{193,65... | collective-permute-start | bytes 589832 | tf_op jit(solution)/shard_map/ppermute | solution.py:19
  17.4 0.8 reduce-window.8
  18.3 0.1 add_bitcast_fusion
  18.3 3.8 %copy.29 = bf16[2,4,2,128,768]{4,3,2,1,0:T(8,128)(2,1)} copy(bf16[2,4,2,128,768]{4,3,0,1,2:T(8,128)(2,1)} %bitcast.86) | data formatting | bytes 6291456 | tf_op jit(solution)/shard_map/transpose | solution.py:101
  22.2 0.1 convert_reduce_fusion
  22.3 1.1 collective-permute-start.3
  23.5 0.1 convert_reduce_fusion.1
  23.6 2.9 %collective-permute-done.8 = bf16[128,768]{1,0:T(8,128)(2,1)S(1)} collective-permute-done((bf16[128,768]{1,0:T(8,128)(2,1)}, bf16[128,768]{1,0:T(8,128)(2,1)S(1)}, u32[]{:S(2)}, u32[]{:S(2)}) %collective-permute-start.8) | collective-permute-done | bytes 196640 | tf_op jit(solution)/shard_map/ppermute | solution.py:19
  26.5 6.1 %collective-permute-start.2 = (bf16[512,256]{1,0:T(8,128)(2,1)S(1)}, bf16[512,256]{1,0:T(8,128)(2,1)S(1)}, u32[]{:S(2)}, u32[]{:S(2)}) collective-permute-start(bf16[512,256]{1,0:T(8,128)(2,1)S(1)} %constant_dynamic-update-slice_fusion), channel_id=1, source_target_pairs={{0,3},{4,7},{8,11},{12,15},{16,19},{20,23},{24,27},{28,31},{32,35}... | collective-permute-start | bytes 786440 | tf_op jit(solution)/shard_map/ppermute | solution.py:23
  32.6 1.3 collective-permute-start.1
  33.9 2.2 %collective-permute-start = (bf16[512,256]{1,0:T(8,128)(2,1)S(1)}, bf16[512,256]{1,0:T(8,128)(2,1)S(1)}, u32[]{:S(2)}, u32[]{:S(2)}) collective-permute-start(bf16[512,256]{1,0:T(8,128)(2,1)S(1)} %constant_dynamic-update-slice_fusion), channel_id=1, source_target_pairs={{0,1},{1,2},{2,3},{4,5},{5,6},{6,7},{8,9},{9,10},{10,11},{12,13},{... | collective-permute-start | bytes 786440 | tf_op jit(solution)/shard_map/ppermute | solution.py:23
  36.1 0.2 fusion.7
  36.3 3.7 %convolution_convert_fusion = bf16[512,2048]{1,0:T(8,128)(2,1)S(1)} fusion(bf16[512,768]{1,0:T(8,128)(2,1)S(1)} %bitcast.89, bf16[2048,768]{1,0:T(8,128)(2,1)} %bitcast.87), kind=kOutput, calls=%fused_computation.8 | convolution fusion | flops 1611661312 | bytes 6029312 | tf_op jit(solution)/shard_map/tf,hf->th/dot_general | solution.py:104
  40.1 0.1 constant_dynamic-slice_fusion.4
  40.2 2.2 %collective-permute-start.6 = (bf16[512,1024]{1,0:T(8,128)(2,1)S(1)}, bf16[512,1024]{1,0:T(8,128)(2,1)}, u32[]{:S(2)}, u32[]{:S(2)}) collective-permute-start(bf16[512,1024]{1,0:T(8,128)(2,1)S(1)} %constant_dynamic-slice_fusion.4), channel_id=1, source_target_pairs={{0,4},{4,0},{1,5},{5,1},{2,6},{6,2},{3,7},{7,3},{8,12},{12,8},{9,1... | collective-permute-start | bytes 3145736 | tf_op jit(solution)/shard_map/ppermute | solution.py:19
  42.4 5.6 %collective-permute-done = bf16[512,256]{1,0:T(8,128)(2,1)S(1)} collective-permute-done((bf16[512,256]{1,0:T(8,128)(2,1)S(1)}, bf16[512,256]{1,0:T(8,128)(2,1)S(1)}, u32[]{:S(2)}, u32[]{:S(2)}) %collective-permute-start) | collective-permute-done | bytes 262176 | tf_op jit(solution)/shard_map/ppermute | solution.py:23
  47.9 0.1 pad_maximum_fusion.1
  48.1 1.6 fusion
  49.7 1.7 fusion.26
  51.4 2.0 %copy-done = f32[512,2048]{1,0:T(8,128)} copy-done((f32[512,2048]{1,0:T(8,128)}, f32[512,2048]{1,0:T(8,128)S(1)}, u32[]{:S(2)}) %copy-start) | copy-done | bytes 4194328
  53.4 1.4 convolution_convert_fusion.2
  54.8 1.9 %add_convert_fusion = bf16[512,1024]{1,0:T(8,128)(2,1)S(1)} fusion(bf16[512,1024]{1,0:T(8,128)(2,1)} %collective-permute-done.6, bf16[512,2048]{1,0:T(8,128)(2,1)} %copy-done.3, s32[]{:T(128)S(6)} %select_n.99), kind=kLoop, calls=%fused_computation.20 | loop fusion | flops 2097152 | bytes 3145732 | tf_op jit(solution)/shard_map/convert_element_type | solution.py:107
  56.9 1.0 constant_dynamic-slice_fusion.3
  57.8 1.2 collective-permute-start.13
  59.0 1.5 collective-permute-start.15
  60.5 1.5 collective-permute-start.14
  62.0 2.4 %collective-permute-done.13 = bf16[512,256]{1,0:T(8,128)(2,1)S(1)} collective-permute-done((bf16[512,256]{1,0:T(8,128)(2,1)}, bf16[512,256]{1,0:T(8,128)(2,1)S(1)}, u32[]{:S(2)}, u32[]{:S(2)}) %collective-permute-start.13) | collective-permute-done | bytes 262176 | tf_op jit(solution)/shard_map/ppermute | solution.py:19
  64.5 0.2 collective-permute-done.15
  64.7 6.3 %collective-permute-done.14 = bf16[512,256]{1,0:T(8,128)(2,1)} collective-permute-done((bf16[512,256]{1,0:T(8,128)(2,1)S(1)}, bf16[512,256]{1,0:T(8,128)(2,1)}, u32[]{:S(2)}, u32[]{:S(2)}) %collective-permute-start.14) | collective-permute-done | bytes 262176 | tf_op jit(solution)/shard_map/ppermute | solution.py:19
  71.0 1.2 add_convert_fusion.2
  72.2 5.2 %collective-permute-start.16 = (bf16[512,128]{1,0:T(8,128)(2,1)S(1)}, bf16[512,128]{1,0:T(8,128)(2,1)S(1)}, u32[]{:S(2)}, u32[]{:S(2)}) collective-permute-start(bf16[512,128]{1,0:T(8,128)(2,1)S(1)} %constant_dynamic-slice_fusion), channel_id=1, source_target_pairs={{0,32},{32,0},{1,33},{33,1},{2,34},{34,2},{3,35},{35,3},{4,36},{36... | collective-permute-start | bytes 393224 | tf_op jit(solution)/shard_map/ppermute | solution.py:19
  77.4 2.6 %collective-permute-done.16 = bf16[512,128]{1,0:T(8,128)(2,1)S(1)} collective-permute-done((bf16[512,128]{1,0:T(8,128)(2,1)S(1)}, bf16[512,128]{1,0:T(8,128)(2,1)S(1)}, u32[]{:S(2)}, u32[]{:S(2)}) %collective-permute-start.16) | collective-permute-done | bytes 131104 | tf_op jit(solution)/shard_map/ppermute | solution.py:19
  80.0 3.0 %multiply_reduce_fusion = (f32[512]{0:T(512)S(1)}, f32[512,2048]{1,0:T(8,128)S(1)}) fusion(f32[512,2048]{1,0:T(8,128)} %copy-done, f32[512]{0:T(512)S(1)} %broadcast_divide_fusion, bf16[2048,256]{1,0:T(8,128)(2,1)S(1)} %bitcast.80, bf16[512,128]{1,0:T(8,128)(2,1)S(1)} %collective-permute-done.16, bf16[512,256]{1,0:T(8,128)(2,1)S(1)} %add_convert_fusion.2, ...), kind=kOutput, calls=%fused_computation.1 | convolution fusion | flops 271842816 | bytes 9179140 | tf_op jit(solution)/shard_map/dot_general | solution.py:116
  83.0 0.6 multiply_convert_fusion
  83.6 0.9 fusion.1
  84.5 0.6 convolution_convert_fusion.1
  85.2 1.3 collective-permute-start.17
  86.5 1.2 fusion.8
  87.7 2.7 %collective-permute-start.10 = (bf16[4,128,768]{2,1,0:T(8,128)(2,1)}, bf16[4,128,768]{2,1,0:T(8,128)(2,1)S(1)}, u32[]{:S(2)}, u32[]{:S(2)}) collective-permute-start(bf16[4,128,768]{2,1,0:T(8,128)(2,1)} %fusion.8), channel_id=1, source_target_pairs={{0,192},{64,0},{128,64},{192,128},{1,193},{65,1},{129,65},{193,129... | collective-permute-start | bytes 2359304 | tf_op jit(solution)/shard_map/ppermute | solution.py:19
  90.4 0.4 collective-permute-start.11
  90.8 0.7 collective-permute-start.12
  91.4 0.3 fusion.37
  91.7 1.3 collective-permute-start.19
  93.0 13.5 %collective-permute-done.17 = bf16[512,256]{0,1:T(8,128)(2,1)S(1)} collective-permute-done((bf16[512,256]{0,1:T(8,128)(2,1)S(1)}, bf16[512,256]{0,1:T(8,128)(2,1)S(1)}, u32[]{:S(2)}, u32[]{:S(2)}) %collective-permute-start.17) | collective-permute-done | bytes 262176 | tf_op jit(solution)/shard_map/ppermute | solution.py:23
  106.5 1.5 collective-permute-start.18
  108.0 0.7 fusion.3
  108.7 1.2 fusion.18
  109.9 3.1 %collective-permute-done.19 = bf16[512,256]{0,1:T(8,128)(2,1)S(1)} collective-permute-done((bf16[512,256]{0,1:T(8,128)(2,1)S(1)}, bf16[512,256]{0,1:T(8,128)(2,1)S(1)}, u32[]{:S(2)}, u32[]{:S(2)}) %collective-permute-start.19) | collective-permute-done | bytes 262176 | tf_op jit(solution)/shard_map/ppermute | solution.py:23
  113.0 19.4 %collective-permute-done.18 = bf16[512,256]{0,1:T(8,128)(2,1)S(1)} collective-permute-done((bf16[512,256]{0,1:T(8,128)(2,1)S(1)}, bf16[512,256]{0,1:T(8,128)(2,1)S(1)}, u32[]{:S(2)}, u32[]{:S(2)}) %collective-permute-start.18) | collective-permute-done | bytes 262176 | tf_op jit(solution)/shard_map/ppermute | solution.py:23
  132.4 0.2 add_convert_fusion.1
  132.6 0.8 copy.35
  133.3 0.8 copy.34
  134.1 1.6 pad_maximum_fusion
  135.7 0.3 fusion.27
  136.0 18.1 %all-gather.3.cloned.1.call-done = bf16[32768,128]{1,0:T(8,128)(2,1)} async-done(((bf16[512,128]{1,0:T(8,128)(2,1)}), bf16[32768,128]{1,0:T(8,128)(2,1)}) %all-gather.3.cloned.1.call-update) | async-done | bytes 8388624 | tf_op jit(solution)/shard_map/all_gather | solution.py:111
  154.1 3.6 %fusion.2 = f32[2,4,2,128,768]{4,3,2,1,0:T(8,128)S(1)} fusion(bf16[512,768,1,1,1]{1,0,4,3,2:T(8,128)(2,1)S(1)} %bitcast.85, bf16[2,4,4,2,512,128]{5,4,3,2,1,0:T(8,128)(2,1)} %bitcast.73), kind=kOutput, calls=%fused_computation.19 | convolution fusion | flops 1610612736 | bytes 9175040 | tf_op jit(solution)/shard_map/zxcth,tf->zxchf/dot_general | solution.py:139
  157.6 0.4 copy-done.2
  158.1 1.8 %convolution_add_fusion.2 = f32[2,4,2,128,768]{4,3,2,1,0:T(8,128)S(1)} fusion(f32[2,4,2,128,768]{4,3,2,1,0:T(8,128)S(1)} %fusion.2, bf16[512,768,1,1,1]{1,0,4,3,2:T(8,128)(2,1)S(1)} %bitcast.84, bf16[2,4,4,2,512,128]{5,4,3,2,1,0:T(8,128)(2,1)S(1)} %bitcast.74), kind=kOutput, calls=%fused_computation.11 | convolution fusion | flops 1612185600 | bytes 15466496 | tf_op jit(solution)/shard_map/zxcth,tf->zxchf/dot_general | solution.py:139
  159.9 1.8 %convolution_add_fusion.1 = f32[2,4,2,128,768]{4,3,2,1,0:T(8,128)S(1)} fusion(f32[2,4,2,128,768]{4,3,2,1,0:T(8,128)S(1)} %convolution_add_fusion.2, bf16[512,768,1,1,1]{1,0,4,3,2:T(8,128)(2,1)S(1)} %bitcast.83, bf16[2,4,4,2,512,128]{5,4,3,2,1,0:T(8,128)(2,1)S(1)} %bitcast.75), kind=kOutput, calls=%fused_computation.10 | convolution fusion | flops 1612185600 | bytes 15466496 | tf_op jit(solution)/shard_map/zxcth,tf->zxchf/dot_general | solution.py:139
  161.7 4.5 %convolution_add_fusion = f32[2,4,2,128,768]{4,3,2,1,0:T(8,128)} fusion(f32[2,4,2,128,768]{4,3,2,1,0:T(8,128)S(1)} %convolution_add_fusion.1, bf16[512,768,1,1,1]{1,0,4,3,2:T(8,128)(2,1)S(1)} %bitcast.82, bf16[2,4,4,2,512,128]{5,4,3,2,1,0:T(8,128)(2,1)S(1)} %bitcast.76), kind=kOutput, calls=%fused_computation.9 | convolution fusion | flops 1612185600 | bytes 15466496 | tf_op jit(solution)/shard_map/zxcth,tf->zxchf/dot_general | solution.py:139
  (36 shorter events, 0.3 us)
Async XLA Ops:
  7.2 15.2 %copy-start.4 = (bf16[1,128,768]{2,1,0:T(8,128)(2,1)S(1)}, bf16[1,128,768]{2,1,0:T(8,128)(2,1)}, u32[]{:S(2)}) copy-start(bf16[1,128,768]{2,1,0:T(8,128)(2,1)} %param.6) | copy-start | bytes 589828
  7.2 15.1 %copy-start.5 = (bf16[512,128]{1,0:T(8,128)(2,1)S(1)}, bf16[512,128]{1,0:T(8,128)(2,1)}, u32[]{:S(2)}) copy-start(bf16[512,128]{1,0:T(8,128)(2,1)} %param.9) | copy-start | bytes 393220
  7.2 16.4 %copy-start.6 = (bf16[512,128]{1,0:T(8,128)(2,1)S(1)}, bf16[512,128]{1,0:T(8,128)(2,1)}, u32[]{:S(2)}) copy-start(bf16[512,128]{1,0:T(8,128)(2,1)} %param.10) | copy-start | bytes 393220
  7.2 146.9 %all-gather.3.cloned.1.call-start = ((), (), s32[]{:S(2)}) async-start(), calls=%async_computation | async-start | bytes 8519680 | tf_op jit(solution)/shard_map/all_gather | solution.py:111
  7.2 15.1 %collective-permute-start.9 = (bf16[128,768]{1,0:T(8,128)(2,1)}, bf16[128,768]{1,0:T(8,128)(2,1)S(1)}, u32[]{:S(2)}, u32[]{:S(2)}) collective-permute-start(bf16[128,768]{1,0:T(8,128)(2,1)} %bitcast.94), channel_id=1, source_target_pairs={{0,1},{1,2},{2,3},{3,0},{4,5},{5,6},{6,7},{7,4},{8,9},{9,10},{10,1... | collective-permute-start | bytes 589832 | tf_op jit(solution)/shard_map/ppermute | solution.py:19
  9.8 16.7 %collective-permute-start.8 = (bf16[128,768]{1,0:T(8,128)(2,1)}, bf16[128,768]{1,0:T(8,128)(2,1)S(1)}, u32[]{:S(2)}, u32[]{:S(2)}) collective-permute-start(bf16[128,768]{1,0:T(8,128)(2,1)} %bitcast.95), channel_id=1, source_target_pairs={{0,2},{1,3},{2,0},{3,1},{4,6},{5,7},{6,4},{7,5},{8,10},{9,11},{10,... | collective-permute-start | bytes 589832 | tf_op jit(solution)/shard_map/ppermute | solution.py:19
  12.8 19.8 %collective-permute-start.7 = (bf16[128,768]{1,0:T(8,128)(2,1)}, bf16[128,768]{1,0:T(8,128)(2,1)S(1)}, u32[]{:S(2)}, u32[]{:S(2)}) collective-permute-start(bf16[128,768]{1,0:T(8,128)(2,1)} %bitcast.96), channel_id=1, source_target_pairs={{0,3},{1,0},{2,1},{3,2},{4,7},{5,4},{6,5},{7,6},{8,11},{9,8},{10,9... | collective-permute-start | bytes 589832 | tf_op jit(solution)/shard_map/ppermute | solution.py:19
  13.5 20.4 %collective-permute-start.5 = (bf16[128,768]{1,0:T(8,128)(2,1)}, bf16[128,768]{1,0:T(8,128)(2,1)S(1)}, u32[]{:S(2)}, u32[]{:S(2)}) collective-permute-start(bf16[128,768]{1,0:T(8,128)(2,1)} %bitcast.97), channel_id=1, source_target_pairs={{0,64},{64,128},{128,192},{192,0},{1,65},{65,129},{129,193},{193,1... | collective-permute-start | bytes 589832 | tf_op jit(solution)/shard_map/ppermute | solution.py:19
  14.8 21.3 %collective-permute-start.4 = (bf16[128,768]{1,0:T(8,128)(2,1)}, bf16[128,768]{1,0:T(8,128)(2,1)S(1)}, u32[]{:S(2)}, u32[]{:S(2)}) collective-permute-start(bf16[128,768]{1,0:T(8,128)(2,1)} %bitcast.98), channel_id=1, source_target_pairs={{0,128},{64,192},{128,0},{192,64},{1,129},{65,193},{129,1},{193,65... | collective-permute-start | bytes 589832 | tf_op jit(solution)/shard_map/ppermute | solution.py:19
  22.3 13.8 %collective-permute-start.3 = (bf16[128,768]{1,0:T(8,128)(2,1)S(1)}, bf16[128,768]{1,0:T(8,128)(2,1)S(1)}, u32[]{:S(2)}, u32[]{:S(2)}) collective-permute-start(bf16[128,768]{1,0:T(8,128)(2,1)S(1)} %bitcast.99), channel_id=1, source_target_pairs={{0,192},{64,0},{128,64},{192,128},{1,193},{65,1},{129,65},{193,129... | collective-permute-start | bytes 589832 | tf_op jit(solution)/shard_map/ppermute | solution.py:19
  26.5 15.9 %collective-permute-start.2 = (bf16[512,256]{1,0:T(8,128)(2,1)S(1)}, bf16[512,256]{1,0:T(8,128)(2,1)S(1)}, u32[]{:S(2)}, u32[]{:S(2)}) collective-permute-start(bf16[512,256]{1,0:T(8,128)(2,1)S(1)} %constant_dynamic-update-slice_fusion), channel_id=1, source_target_pairs={{0,3},{4,7},{8,11},{12,15},{16,19},{20,23},{24,27},{28,31},{32,35}... | collective-permute-start | bytes 786440 | tf_op jit(solution)/shard_map/ppermute | solution.py:23
  32.6 9.8 %collective-permute-start.1 = (bf16[512,256]{1,0:T(8,128)(2,1)S(1)}, bf16[512,256]{1,0:T(8,128)(2,1)S(1)}, u32[]{:S(2)}, u32[]{:S(2)}) collective-permute-start(bf16[512,256]{1,0:T(8,128)(2,1)S(1)} %constant_dynamic-update-slice_fusion), channel_id=1, source_target_pairs={{0,2},{1,3},{4,6},{5,7},{8,10},{9,11},{12,14},{13,15},{16,18},{17,... | collective-permute-start | bytes 786440 | tf_op jit(solution)/shard_map/ppermute | solution.py:23
  33.9 14.0 %collective-permute-start = (bf16[512,256]{1,0:T(8,128)(2,1)S(1)}, bf16[512,256]{1,0:T(8,128)(2,1)S(1)}, u32[]{:S(2)}, u32[]{:S(2)}) collective-permute-start(bf16[512,256]{1,0:T(8,128)(2,1)S(1)} %constant_dynamic-update-slice_fusion), channel_id=1, source_target_pairs={{0,1},{1,2},{2,3},{4,5},{5,6},{6,7},{8,9},{9,10},{10,11},{12,13},{... | collective-permute-start | bytes 786440 | tf_op jit(solution)/shard_map/ppermute | solution.py:23
  40.0 8.0 %copy-start.3 = (bf16[512,2048]{1,0:T(8,128)(2,1)}, bf16[512,2048]{1,0:T(8,128)(2,1)S(1)}, u32[]{:S(2)}) copy-start(bf16[512,2048]{1,0:T(8,128)(2,1)S(1)} %convolution_convert_fusion) | copy-start | bytes 6291460
  40.0 8.0 %copy-start.7 = (bf16[512,128]{1,0:T(8,128)(2,1)S(1)}, bf16[512,128]{1,0:T(8,128)(2,1)}, u32[]{:S(2)}) copy-start(bf16[512,128]{1,0:T(8,128)(2,1)} %param.8) | copy-start | bytes 393220
  40.2 14.7 %collective-permute-start.6 = (bf16[512,1024]{1,0:T(8,128)(2,1)S(1)}, bf16[512,1024]{1,0:T(8,128)(2,1)}, u32[]{:S(2)}, u32[]{:S(2)}) collective-permute-start(bf16[512,1024]{1,0:T(8,128)(2,1)S(1)} %constant_dynamic-slice_fusion.4), channel_id=1, source_target_pairs={{0,4},{4,0},{1,5},{5,1},{2,6},{6,2},{3,7},{7,3},{8,12},{12,8},{9,1... | collective-permute-start | bytes 3145736 | tf_op jit(solution)/shard_map/ppermute | solution.py:19
  51.4 2.0 %copy-start = (f32[512,2048]{1,0:T(8,128)}, f32[512,2048]{1,0:T(8,128)S(1)}, u32[]{:S(2)}) copy-start(f32[512,2048]{1,0:T(8,128)S(1)} %get-tuple-element.27) | copy-start | bytes 12582916
  57.8 6.6 %collective-permute-start.13 = (bf16[512,256]{1,0:T(8,128)(2,1)}, bf16[512,256]{1,0:T(8,128)(2,1)S(1)}, u32[]{:S(2)}, u32[]{:S(2)}) collective-permute-start(bf16[512,256]{1,0:T(8,128)(2,1)} %get-tuple-element.35), channel_id=1, source_target_pairs={{0,8},{8,16},{16,24},{24,0},{1,9},{9,17},{17,25},{25,1},{2,10},{10... | collective-permute-start | bytes 786440 | tf_op jit(solution)/shard_map/ppermute | solution.py:19
  59.0 5.6 %collective-permute-start.15 = (bf16[512,256]{1,0:T(8,128)(2,1)}, bf16[512,256]{1,0:T(8,128)(2,1)}, u32[]{:S(2)}, u32[]{:S(2)}) collective-permute-start(bf16[512,256]{1,0:T(8,128)(2,1)} %get-tuple-element.36), channel_id=1, source_target_pairs={{0,24},{8,0},{16,8},{24,16},{1,25},{9,1},{17,9},{25,17},{2,26},{10... | collective-permute-start | bytes 786440 | tf_op jit(solution)/shard_map/ppermute | solution.py:19
  60.5 10.5 %collective-permute-start.14 = (bf16[512,256]{1,0:T(8,128)(2,1)S(1)}, bf16[512,256]{1,0:T(8,128)(2,1)}, u32[]{:S(2)}, u32[]{:S(2)}) collective-permute-start(bf16[512,256]{1,0:T(8,128)(2,1)S(1)} %get-tuple-element.37), channel_id=1, source_target_pairs={{0,16},{8,24},{16,0},{24,8},{1,17},{9,25},{17,1},{25,9},{2,18},{10... | collective-permute-start | bytes 786440 | tf_op jit(solution)/shard_map/ppermute | solution.py:19
  72.2 7.8 %collective-permute-start.16 = (bf16[512,128]{1,0:T(8,128)(2,1)S(1)}, bf16[512,128]{1,0:T(8,128)(2,1)S(1)}, u32[]{:S(2)}, u32[]{:S(2)}) collective-permute-start(bf16[512,128]{1,0:T(8,128)(2,1)S(1)} %constant_dynamic-slice_fusion), channel_id=1, source_target_pairs={{0,32},{32,0},{1,33},{33,1},{2,34},{34,2},{3,35},{35,3},{4,36},{36... | collective-permute-start | bytes 393224 | tf_op jit(solution)/shard_map/ppermute | solution.py:19
  77.4 5.6 %copy-start.1 = (f32[512,2048]{1,0:T(8,128)S(1)}, f32[512,2048]{1,0:T(8,128)}, u32[]{:S(2)}) copy-start(f32[512,2048]{1,0:T(8,128)} %copy-done) | copy-start | bytes 12582916
  85.2 21.3 %collective-permute-start.17 = (bf16[512,256]{0,1:T(8,128)(2,1)S(1)}, bf16[512,256]{0,1:T(8,128)(2,1)S(1)}, u32[]{:S(2)}, u32[]{:S(2)}) collective-permute-start(bf16[512,256]{0,1:T(8,128)(2,1)S(1)} %get-tuple-element.32), channel_id=1, source_target_pairs={{1,0},{2,1},{3,2},{5,4},{6,5},{7,6},{9,8},{10,9},{11,10},{13,12},{... | collective-permute-start | bytes 786440 | tf_op jit(solution)/shard_map/ppermute | solution.py:23
  87.7 46.4 %collective-permute-start.10 = (bf16[4,128,768]{2,1,0:T(8,128)(2,1)}, bf16[4,128,768]{2,1,0:T(8,128)(2,1)S(1)}, u32[]{:S(2)}, u32[]{:S(2)}) collective-permute-start(bf16[4,128,768]{2,1,0:T(8,128)(2,1)} %fusion.8), channel_id=1, source_target_pairs={{0,192},{64,0},{128,64},{192,128},{1,193},{65,1},{129,65},{193,129... | collective-permute-start | bytes 2359304 | tf_op jit(solution)/shard_map/ppermute | solution.py:19
  90.4 43.7 %collective-permute-start.11 = (bf16[4,128,768]{2,1,0:T(8,128)(2,1)}, bf16[4,128,768]{2,1,0:T(8,128)(2,1)}, u32[]{:S(2)}, u32[]{:S(2)}) collective-permute-start(bf16[4,128,768]{2,1,0:T(8,128)(2,1)} %fusion.8), channel_id=1, source_target_pairs={{0,128},{64,192},{128,0},{192,64},{1,129},{65,193},{129,1},{193,65... | collective-permute-start | bytes 2359304 | tf_op jit(solution)/shard_map/ppermute | solution.py:19
  90.8 43.3 %collective-permute-start.12 = (bf16[4,128,768]{2,1,0:T(8,128)(2,1)}, bf16[4,128,768]{2,1,0:T(8,128)(2,1)}, u32[]{:S(2)}, u32[]{:S(2)}) collective-permute-start(bf16[4,128,768]{2,1,0:T(8,128)(2,1)} %fusion.8), channel_id=1, source_target_pairs={{0,64},{64,128},{128,192},{192,0},{1,65},{65,129},{129,193},{193,1... | collective-permute-start | bytes 2359304 | tf_op jit(solution)/shard_map/ppermute | solution.py:19
  91.7 21.3 %collective-permute-start.19 = (bf16[512,256]{0,1:T(8,128)(2,1)S(1)}, bf16[512,256]{0,1:T(8,128)(2,1)S(1)}, u32[]{:S(2)}, u32[]{:S(2)}) collective-permute-start(bf16[512,256]{0,1:T(8,128)(2,1)S(1)} %get-tuple-element.33), channel_id=1, source_target_pairs={{3,0},{7,4},{11,8},{15,12},{19,16},{23,20},{27,24},{31,28},{35,32}... | collective-permute-start | bytes 786440 | tf_op jit(solution)/shard_map/ppermute | solution.py:23
  106.5 25.9 %collective-permute-start.18 = (bf16[512,256]{0,1:T(8,128)(2,1)S(1)}, bf16[512,256]{0,1:T(8,128)(2,1)S(1)}, u32[]{:S(2)}, u32[]{:S(2)}) collective-permute-start(bf16[512,256]{0,1:T(8,128)(2,1)S(1)} %get-tuple-element.34), channel_id=1, source_target_pairs={{2,0},{3,1},{6,4},{7,5},{10,8},{11,9},{14,12},{15,13},{18,16},{19,... | collective-permute-start | bytes 786440 | tf_op jit(solution)/shard_map/ppermute | solution.py:23
  154.0 4.0 %copy-start.2 = (bf16[32768,128]{1,0:T(8,128)(2,1)S(1)}, bf16[32768,128]{1,0:T(8,128)(2,1)}, u32[]{:S(2)}) copy-start(bf16[32768,128]{1,0:T(8,128)(2,1)} %all-gather.3.cloned.1.call-done) | copy-start | bytes 25165828
Sparse Core Ops, SparseCore 0:
  56.9 97.0 all-gather.2
where the time goes:
time: 174 us; the launch traced here: 173 us
  waiting for transfers between devices  74.1 us (43%)
  starting transfers between devices  40.4 us (23%)
  matrix products  23.8 us (14%)
  between operations  14.4 us (8%)
  other arithmetic  11.2 us (6%)
  local copies, waits for them, and re-layouts  9.22 us (5%)
    ppermute x6, waiting for transfers between devices, shift_open(): lax.ppermute(x, axis, [(i, i + s) for i in range(n) if 0 <= i + s < n])  41.5 us
    ppermute x14, starting transfers between devices, shift(): return lax.ppermute(x, axis, [(i, (i + s) % n) for i in range(n)])  26.7 us
    all_gather x1, waiting for transfers between devices, shards(): lax.all_gather(context[None], ('zh', DEP, 'x', 'core'), axis=0, tiled=True)  18.1 us
    ppermute x14, waiting for transfers between devices, shift(): return lax.ppermute(x, axis, [(i, (i + s) % n) for i in range(n)])  14.5 us
    ppermute x6, starting transfers between devices, shift_open(): lax.ppermute(x, axis, [(i, i + s) for i in range(n) if 0 <= i + s < n])  13.7 us
    dot_general x4, matrix products, shards(): jnp.einsum('zxcth,tf->zxchf', ctx_all[:, depth], rows_all[depth].reshape(...  11.8 us
    unnamed x20, local copies, waits for them, and re-layouts  4.01 us
    transpose x1, local copies, waits for them, and re-layouts, shards(): jnp.transpose(out_weight.reshape(n_zh, n_x, n_core, head_dim, feat), (2,...  3.83 us
  transfers between devices with their start and end apart: 21, of which 10 were waited for; matrix products, arithmetic and copies ran while one was open for 16% of the time, Pallas kernels for 0%

commit v1 on v0

--- a/solution.py
+++ b/solution.py
@@ -108,7 +108,9 @@
         context, partial, by_depth = lax.optimization_barrier((context, partial, by_depth))
         by_depth = roll_rows(by_depth, me_d, 0)
         rows_all = rolled_gather(by_depth, "row", n_row, stack_axis=1)
-        ctx_all = lax.all_gather(context[None], ("zh", DEP, "x", "core"), axis=0, tiled=True)
+        own = context[None]
+        stack = jnp.stack([own] * lax.axis_size(("zh", DEP, "x", "core")))
+        ctx_all = jnp.concatenate(lax.all_to_all(stack, ("zh", DEP, "x", "core"), 0, 0), axis=0)
         ctx_all = ctx_all.reshape(n_zh, n_dep, n_x, n_core, tok_depth, head_dim)
         partial = pp_reduce_scatter_cols(partial, "x", n_x).astype(jnp.bfloat16)
         partial = pp_reduce_scatter_cols(partial, "zh", n_zh).astype(jnp.bfloat16)

time: 174 us -> 331 us (1.90); the launches traced: 173 us -> 326 us
  waiting for transfers between devices: 74.1 us -> 209 us
  starting transfers between devices: 40.4 us -> 64.8 us
  between operations: 14.4 us -> 1.05 us
  local copies, waits for them, and re-layouts: 9.22 us -> 14 us
  matrix products: 23.8 us -> 27.7 us
    ppermute x14, waiting for transfers between devices: 14.5 us -> 182 us  [shift(): return lax.ppermute(x, axis, [(i, (i + s) % n) for i in range(n)])]
    all_to_all x0 -> x1, starting transfers between devices: none -> 19.1 us  [shards(): lax.all_to_all(stack, ('zh', DEP, 'x', 'core'), 0, 0)]
    all_gather x1 -> x0, waiting for transfers between devices: 18.1 us -> none  [shards(): lax.all_gather(context[None], ('zh', DEP, 'x', 'core'), axis=0, tiled=True)]
    ppermute x6, waiting for transfers between devices: 41.5 us -> 26.5 us  [shift_open(): lax.ppermute(x, axis, [(i, i + s) for i in range(n) if 0 <= i + s < n])]
    ppermute x14, starting transfers between devices: 26.7 us -> 32 us  [shift(): return lax.ppermute(x, axis, [(i, (i + s) % n) for i in range(n)])]
    another operation x0 -> x1, local copies, waits for them, and re-layouts: none -> 5.27 us  [shards(): stack = jnp.stack([own] * lax.axis_size(('zh', DEP, 'x', 'core')))]
    dot_general x4, matrix products: 11.8 us -> 16.4 us  [shards(): jnp.einsum('zxcth,tf->zxchf', ctx_all[:, depth], rows_all[depth].reshape(...]
  transfers between devices with their start and end apart: 21 -> 21, of which waited for: 10 -> 10; matrix products, arithmetic and copies ran while one was open for 16% -> 8% of each run, Pallas kernels for 0% -> 0%
where the time goes in v1:
time: 331 us; the launch traced here: 326 us
  waiting for transfers between devices  209 us (63%)
  starting transfers between devices  64.8 us (20%)
  matrix products  27.7 us (8%)
  local copies, waits for them, and re-layouts  14 us (4%)
  other arithmetic  9.67 us (3%)
    ppermute x14, waiting for transfers between devices, shift(): return lax.ppermute(x, axis, [(i, (i + s) % n) for i in range(n)])  182 us
    ppermute x14, starting transfers between devices, shift(): return lax.ppermute(x, axis, [(i, (i + s) % n) for i in range(n)])  32 us
    ppermute x6, waiting for transfers between devices, shift_open(): lax.ppermute(x, axis, [(i, i + s) for i in range(n) if 0 <= i + s < n])  26.5 us
    all_to_all x1, starting transfers between devices, shards(): lax.all_to_all(stack, ('zh', DEP, 'x', 'core'), 0, 0)  19.1 us
    dot_general x4, matrix products, shards(): jnp.einsum('zxcth,tf->zxchf', ctx_all[:, depth], rows_all[depth].reshape(...  16.4 us
    ppermute x6, starting transfers between devices, shift_open(): lax.ppermute(x, axis, [(i, i + s) for i in range(n) if 0 <= i + s < n])  13.7 us
  transfers between devices with their start and end apart: 21, of which 10 were waited for; matrix products, arithmetic and copies ran while one was open for 8% of the time, Pallas kernels for 0%

profile of v1, /device:TPU:1, one launch (start us, length us, event | category | flops | bytes accessed | tf_op | source)
XLA Modules:
  0.0 326.1 jit_solution(8723976086212398895)
XLA Ops:
  0.7 2.5 collective-permute-start.9
  3.2 3.0 collective-permute-start.8
  6.2 0.7 collective-permute-start.7
  6.9 1.3 collective-permute-start.5
  8.2 2.6 collective-permute-start.4
  10.8 0.8 reduce-window.8
  11.8 3.8 %copy.32 = bf16[2,4,2,128,768]{4,3,2,1,0:T(8,128)(2,1)} copy(bf16[2,4,2,128,768]{4,3,0,1,2:T(8,128)(2,1)} %bitcast.82) | data formatting | bytes 6291456 | tf_op jit(solution)/shard_map/transpose | solution.py:101
  15.6 0.1 convert_reduce_fusion
  15.8 1.1 collective-permute-start.3
  16.9 0.1 convert_reduce_fusion.1
  17.0 2.9 collective-permute-done.8
  19.9 6.1 %collective-permute-start.2 = (bf16[512,256]{1,0:T(8,128)(2,1)S(1)}, bf16[512,256]{1,0:T(8,128)(2,1)S(1)}, u32[]{:S(2)}, u32[]{:S(2)}) collective-permute-start(bf16[512,256]{1,0:T(8,128)(2,1)S(1)} %constant_dynamic-update-slice_fusion), channel_id=1, source_target_pairs={{0,3},{4,7},{8,11},{12,15},{16,19},{20,23},{24,27},{28,31},{32,35}... | collective-permute-start | bytes 786440 | tf_op jit(solution)/shard_map/ppermute | solution.py:23
  26.0 1.3 collective-permute-start.1
  27.3 2.2 collective-permute-start
  29.5 0.2 fusion.7
  29.7 3.7 %convolution_convert_fusion = bf16[512,2048]{1,0:T(8,128)(2,1)S(1)} fusion(bf16[512,768]{1,0:T(8,128)(2,1)S(1)} %bitcast.85, bf16[2048,768]{1,0:T(8,128)(2,1)} %bitcast.83), kind=kOutput, calls=%fused_computation.8 | convolution fusion | flops 1611661312 | bytes 6029312 | tf_op jit(solution)/shard_map/tf,hf->th/dot_general | solution.py:104
  33.5 0.1 constant_dynamic-slice_fusion.4
  33.6 2.2 collective-permute-start.6
  35.8 5.6 %collective-permute-done = bf16[512,256]{1,0:T(8,128)(2,1)S(1)} collective-permute-done((bf16[512,256]{1,0:T(8,128)(2,1)S(1)}, bf16[512,256]{1,0:T(8,128)(2,1)S(1)}, u32[]{:S(2)}, u32[]{:S(2)}) %collective-permute-start) | collective-permute-done | bytes 262176 | tf_op jit(solution)/shard_map/ppermute | solution.py:23
  41.3 0.1 pad_maximum_fusion.1
  41.5 1.6 fusion
  43.1 1.7 fusion.26
  44.8 2.0 copy-done
  46.8 0.8 convolution_convert_fusion.2
  47.6 0.4 add_convert_fusion
  48.0 5.3 %stack.70 = bf16[64,1,512,128]{3,2,1,0:T(8,128)(2,1)} broadcast(bf16[512,128]{1,0:T(8,128)(2,1)S(1)} %convolution_convert_fusion.2), dimensions={2,3} | broadcast | bytes 8519680 | tf_op jit(solution)/shard_map/stack | solution.py:112
  53.3 19.1 %all-to-all-start = ((bf16[64,1,512,128]{3,2,1,0:T(8,128)(2,1)}), bf16[64,1,512,128]{3,2,1,0:T(8,128)(2,1)}, u32[]{:S(2)}, u32[]{:S(2)}) async-start(bf16[64,1,512,128]{3,2,1,0:T(8,128)(2,1)} %stack.70), calls=%async_computation | async-start | bytes 16777216 | tf_op jit(solution)/shard_map/all_to_all | solution.py:113
  72.4 0.9 constant_dynamic-slice_fusion.3
  73.4 1.4 collective-permute-start.13
  74.8 1.3 collective-permute-start.15
  76.0 1.7 collective-permute-start.14
  77.7 27.3 %collective-permute-done.13 = bf16[512,256]{1,0:T(8,128)(2,1)S(1)} collective-permute-done((bf16[512,256]{1,0:T(8,128)(2,1)}, bf16[512,256]{1,0:T(8,128)(2,1)S(1)}, u32[]{:S(2)}, u32[]{:S(2)}) %collective-permute-start.13) | collective-permute-done | bytes 262176 | tf_op jit(solution)/shard_map/ppermute | solution.py:19
  105.0 3.8 %collective-permute-done.15 = bf16[512,256]{1,0:T(8,128)(2,1)} collective-permute-done((bf16[512,256]{1,0:T(8,128)(2,1)}, bf16[512,256]{1,0:T(8,128)(2,1)}, u32[]{:S(2)}, u32[]{:S(2)}) %collective-permute-start.15) | collective-permute-done | bytes 262176 | tf_op jit(solution)/shard_map/ppermute | solution.py:19
  108.9 6.3 %collective-permute-done.14 = bf16[512,256]{1,0:T(8,128)(2,1)} collective-permute-done((bf16[512,256]{1,0:T(8,128)(2,1)S(1)}, bf16[512,256]{1,0:T(8,128)(2,1)}, u32[]{:S(2)}, u32[]{:S(2)}) %collective-permute-start.14) | collective-permute-done | bytes 262176 | tf_op jit(solution)/shard_map/ppermute | solution.py:19
  115.1 1.2 add_convert_fusion.2
  116.3 10.3 %collective-permute-start.16 = (bf16[512,128]{1,0:T(8,128)(2,1)S(1)}, bf16[512,128]{1,0:T(8,128)(2,1)S(1)}, u32[]{:S(2)}, u32[]{:S(2)}) collective-permute-start(bf16[512,128]{1,0:T(8,128)(2,1)S(1)} %constant_dynamic-slice_fusion), channel_id=1, source_target_pairs={{0,32},{32,0},{1,33},{33,1},{2,34},{34,2},{3,35},{35,3},{4,36},{36... | collective-permute-start | bytes 393224 | tf_op jit(solution)/shard_map/ppermute | solution.py:19
  126.7 132.6 %collective-permute-done.16 = bf16[512,128]{1,0:T(8,128)(2,1)S(1)} collective-permute-done((bf16[512,128]{1,0:T(8,128)(2,1)S(1)}, bf16[512,128]{1,0:T(8,128)(2,1)S(1)}, u32[]{:S(2)}, u32[]{:S(2)}) %collective-permute-start.16) | collective-permute-done | bytes 131104 | tf_op jit(solution)/shard_map/ppermute | solution.py:19
  259.2 3.0 multiply_reduce_fusion
  262.2 0.6 multiply_convert_fusion
  262.8 0.9 fusion.1
  263.7 0.6 convolution_convert_fusion.1
  264.4 1.3 collective-permute-start.17
  265.7 1.2 fusion.8
  266.9 2.7 collective-permute-start.10
  269.7 0.3 collective-permute-start.11
  270.0 0.7 collective-permute-start.12
  270.7 0.3 fusion.37
  271.0 1.3 collective-permute-start.19
  272.3 5.5 %collective-permute-done.17 = bf16[512,256]{0,1:T(8,128)(2,1)S(1)} collective-permute-done((bf16[512,256]{0,1:T(8,128)(2,1)S(1)}, bf16[512,256]{0,1:T(8,128)(2,1)S(1)}, u32[]{:S(2)}, u32[]{:S(2)}) %collective-permute-start.17) | collective-permute-done | bytes 262176 | tf_op jit(solution)/shard_map/ppermute | solution.py:23
  277.8 1.5 collective-permute-start.18
  279.3 0.7 fusion.3
  280.0 1.2 fusion.18
  281.2 1.8 collective-permute-done.19
  283.0 13.6 %collective-permute-done.18 = bf16[512,256]{0,1:T(8,128)(2,1)S(1)} collective-permute-done((bf16[512,256]{0,1:T(8,128)(2,1)S(1)}, bf16[512,256]{0,1:T(8,128)(2,1)S(1)}, u32[]{:S(2)}, u32[]{:S(2)}) %collective-permute-start.18) | collective-permute-done | bytes 262176 | tf_op jit(solution)/shard_map/ppermute | solution.py:23
  296.6 0.2 add_convert_fusion.1
  296.8 0.8 copy.38
  297.6 0.8 copy.37
  298.3 9.5 %collective-permute-done.12 = bf16[4,128,768]{2,1,0:T(8,128)(2,1)} collective-permute-done((bf16[4,128,768]{2,1,0:T(8,128)(2,1)}, bf16[4,128,768]{2,1,0:T(8,128)(2,1)}, u32[]{:S(2)}, u32[]{:S(2)}) %collective-permute-start.12) | collective-permute-done | bytes 786464 | tf_op jit(solution)/shard_map/ppermute | solution.py:19
  307.8 1.6 pad_maximum_fusion
  309.4 0.3 fusion.27
  309.6 3.4 %fusion.2 = f32[2,4,2,128,768]{4,3,2,1,0:T(8,128)S(1)} fusion(bf16[512,768,1,1,1]{1,0,4,3,2:T(8,128)(2,1)S(1)} %bitcast.81, bf16[2,4,4,2,512,128]{5,4,3,2,1,0:T(8,128)(2,1)} %bitcast.18), kind=kOutput, calls=%fused_computation.19 | convolution fusion | flops 1610612736 | bytes 9175040 | tf_op jit(solution)/shard_map/zxcth,tf->zxchf/dot_general | solution.py:141
  313.1 3.4 %convolution_add_fusion.2 = f32[2,4,2,128,768]{4,3,2,1,0:T(8,128)S(1)} fusion(f32[2,4,2,128,768]{4,3,2,1,0:T(8,128)S(1)} %fusion.2, bf16[512,768,1,1,1]{1,0,4,3,2:T(8,128)(2,1)S(1)} %bitcast.80, bf16[2,4,4,2,512,128]{5,4,3,2,1,0:T(8,128)(2,1)} %bitcast.18), kind=kOutput, calls=%fused_computation.11 | convolution fusion | flops 1612185600 | bytes 15466496 | tf_op jit(solution)/shard_map/zxcth,tf->zxchf/dot_general | solution.py:141
  316.5 3.4 %convolution_add_fusion.1 = f32[2,4,2,128,768]{4,3,2,1,0:T(8,128)S(1)} fusion(f32[2,4,2,128,768]{4,3,2,1,0:T(8,128)S(1)} %convolution_add_fusion.2, bf16[512,768,1,1,1]{1,0,4,3,2:T(8,128)(2,1)S(1)} %bitcast.79, bf16[2,4,4,2,512,128]{5,4,3,2,1,0:T(8,128)(2,1)} %bitcast.18), kind=kOutput, calls=%fused_computation.10 | convolution fusion | flops 1612185600 | bytes 15466496 | tf_op jit(solution)/shard_map/zxcth,tf->zxchf/dot_general | solution.py:141
  319.9 6.1 %convolution_add_fusion = f32[2,4,2,128,768]{4,3,2,1,0:T(8,128)} fusion(f32[2,4,2,128,768]{4,3,2,1,0:T(8,128)S(1)} %convolution_add_fusion.1, bf16[512,768,1,1,1]{1,0,4,3,2:T(8,128)(2,1)S(1)} %bitcast.78, bf16[2,4,4,2,512,128]{5,4,3,2,1,0:T(8,128)(2,1)} %bitcast.18), kind=kOutput, calls=%fused_computation.9 | convolution fusion | flops 1612185600 | bytes 15466496 | tf_op jit(solution)/shard_map/zxcth,tf->zxchf/dot_general | solution.py:141
  (32 shorter events, 0.3 us)
Async XLA Ops:
  0.6 15.1 %copy-start.2 = (bf16[1,128,768]{2,1,0:T(8,128)(2,1)S(1)}, bf16[1,128,768]{2,1,0:T(8,128)(2,1)}, u32[]{:S(2)}) copy-start(bf16[1,128,768]{2,1,0:T(8,128)(2,1)} %param.6) | copy-start | bytes 589828
  0.6 15.1 %copy-start.3 = (bf16[512,128]{1,0:T(8,128)(2,1)S(1)}, bf16[512,128]{1,0:T(8,128)(2,1)}, u32[]{:S(2)}) copy-start(bf16[512,128]{1,0:T(8,128)(2,1)} %param.9) | copy-start | bytes 393220
  0.7 16.3 %copy-start.4 = (bf16[512,128]{1,0:T(8,128)(2,1)S(1)}, bf16[512,128]{1,0:T(8,128)(2,1)}, u32[]{:S(2)}) copy-start(bf16[512,128]{1,0:T(8,128)(2,1)} %param.10) | copy-start | bytes 393220
  0.7 15.1 %collective-permute-start.9 = (bf16[128,768]{1,0:T(8,128)(2,1)}, bf16[128,768]{1,0:T(8,128)(2,1)S(1)}, u32[]{:S(2)}, u32[]{:S(2)}) collective-permute-start(bf16[128,768]{1,0:T(8,128)(2,1)} %bitcast.90), channel_id=1, source_target_pairs={{0,1},{1,2},{2,3},{3,0},{4,5},{5,6},{6,7},{7,4},{8,9},{9,10},{10,1... | collective-permute-start | bytes 589832 | tf_op jit(solution)/shard_map/ppermute | solution.py:19
  3.2 16.7 %collective-permute-start.8 = (bf16[128,768]{1,0:T(8,128)(2,1)}, bf16[128,768]{1,0:T(8,128)(2,1)S(1)}, u32[]{:S(2)}, u32[]{:S(2)}) collective-permute-start(bf16[128,768]{1,0:T(8,128)(2,1)} %bitcast.91), channel_id=1, source_target_pairs={{0,2},{1,3},{2,0},{3,1},{4,6},{5,7},{6,4},{7,5},{8,10},{9,11},{10,... | collective-permute-start | bytes 589832 | tf_op jit(solution)/shard_map/ppermute | solution.py:19
  6.2 19.8 %collective-permute-start.7 = (bf16[128,768]{1,0:T(8,128)(2,1)}, bf16[128,768]{1,0:T(8,128)(2,1)S(1)}, u32[]{:S(2)}, u32[]{:S(2)}) collective-permute-start(bf16[128,768]{1,0:T(8,128)(2,1)} %bitcast.92), channel_id=1, source_target_pairs={{0,3},{1,0},{2,1},{3,2},{4,7},{5,4},{6,5},{7,6},{8,11},{9,8},{10,9... | collective-permute-start | bytes 589832 | tf_op jit(solution)/shard_map/ppermute | solution.py:19
  6.9 20.4 %collective-permute-start.5 = (bf16[128,768]{1,0:T(8,128)(2,1)}, bf16[128,768]{1,0:T(8,128)(2,1)S(1)}, u32[]{:S(2)}, u32[]{:S(2)}) collective-permute-start(bf16[128,768]{1,0:T(8,128)(2,1)} %bitcast.93), channel_id=1, source_target_pairs={{0,64},{64,128},{128,192},{192,0},{1,65},{65,129},{129,193},{193,1... | collective-permute-start | bytes 589832 | tf_op jit(solution)/shard_map/ppermute | solution.py:19
  8.2 21.3 %collective-permute-start.4 = (bf16[128,768]{1,0:T(8,128)(2,1)}, bf16[128,768]{1,0:T(8,128)(2,1)S(1)}, u32[]{:S(2)}, u32[]{:S(2)}) collective-permute-start(bf16[128,768]{1,0:T(8,128)(2,1)} %bitcast.94), channel_id=1, source_target_pairs={{0,128},{64,192},{128,0},{192,64},{1,129},{65,193},{129,1},{193,65... | collective-permute-start | bytes 589832 | tf_op jit(solution)/shard_map/ppermute | solution.py:19
  15.8 13.8 %collective-permute-start.3 = (bf16[128,768]{1,0:T(8,128)(2,1)S(1)}, bf16[128,768]{1,0:T(8,128)(2,1)S(1)}, u32[]{:S(2)}, u32[]{:S(2)}) collective-permute-start(bf16[128,768]{1,0:T(8,128)(2,1)S(1)} %bitcast.95), channel_id=1, source_target_pairs={{0,192},{64,0},{128,64},{192,128},{1,193},{65,1},{129,65},{193,129... | collective-permute-start | bytes 589832 | tf_op jit(solution)/shard_map/ppermute | solution.py:19
  19.9 15.9 %collective-permute-start.2 = (bf16[512,256]{1,0:T(8,128)(2,1)S(1)}, bf16[512,256]{1,0:T(8,128)(2,1)S(1)}, u32[]{:S(2)}, u32[]{:S(2)}) collective-permute-start(bf16[512,256]{1,0:T(8,128)(2,1)S(1)} %constant_dynamic-update-slice_fusion), channel_id=1, source_target_pairs={{0,3},{4,7},{8,11},{12,15},{16,19},{20,23},{24,27},{28,31},{32,35}... | collective-permute-start | bytes 786440 | tf_op jit(solution)/shard_map/ppermute | solution.py:23
  26.0 9.8 %collective-permute-start.1 = (bf16[512,256]{1,0:T(8,128)(2,1)S(1)}, bf16[512,256]{1,0:T(8,128)(2,1)S(1)}, u32[]{:S(2)}, u32[]{:S(2)}) collective-permute-start(bf16[512,256]{1,0:T(8,128)(2,1)S(1)} %constant_dynamic-update-slice_fusion), channel_id=1, source_target_pairs={{0,2},{1,3},{4,6},{5,7},{8,10},{9,11},{12,14},{13,15},{16,18},{17,... | collective-permute-start | bytes 786440 | tf_op jit(solution)/shard_map/ppermute | solution.py:23
  27.3 14.0 %collective-permute-start = (bf16[512,256]{1,0:T(8,128)(2,1)S(1)}, bf16[512,256]{1,0:T(8,128)(2,1)S(1)}, u32[]{:S(2)}, u32[]{:S(2)}) collective-permute-start(bf16[512,256]{1,0:T(8,128)(2,1)S(1)} %constant_dynamic-update-slice_fusion), channel_id=1, source_target_pairs={{0,1},{1,2},{2,3},{4,5},{5,6},{6,7},{8,9},{9,10},{10,11},{12,13},{... | collective-permute-start | bytes 786440 | tf_op jit(solution)/shard_map/ppermute | solution.py:23
  33.5 8.0 %copy-start.5 = (bf16[512,128]{1,0:T(8,128)(2,1)S(1)}, bf16[512,128]{1,0:T(8,128)(2,1)}, u32[]{:S(2)}) copy-start(bf16[512,128]{1,0:T(8,128)(2,1)} %param.8) | copy-start | bytes 393220
  33.6 14.0 %collective-permute-start.6 = (bf16[512,1024]{1,0:T(8,128)(2,1)S(1)}, bf16[512,1024]{1,0:T(8,128)(2,1)S(1)}, u32[]{:S(2)}, u32[]{:S(2)}) collective-permute-start(bf16[512,1024]{1,0:T(8,128)(2,1)S(1)} %constant_dynamic-slice_fusion.4), channel_id=1, source_target_pairs={{0,4},{4,0},{1,5},{5,1},{2,6},{6,2},{3,7},{7,3},{8,12},{12,8},{9,1... | collective-permute-start | bytes 3145736 | tf_op jit(solution)/shard_map/ppermute | solution.py:19
  44.8 2.0 copy-start
  53.3 256.3 %all-to-all-start = ((bf16[64,1,512,128]{3,2,1,0:T(8,128)(2,1)}), bf16[64,1,512,128]{3,2,1,0:T(8,128)(2,1)}, u32[]{:S(2)}, u32[]{:S(2)}) async-start(bf16[64,1,512,128]{3,2,1,0:T(8,128)(2,1)} %stack.70), calls=%async_computation | async-start | bytes 16777216 | tf_op jit(solution)/shard_map/all_to_all | solution.py:113
  73.4 31.7 %collective-permute-start.13 = (bf16[512,256]{1,0:T(8,128)(2,1)}, bf16[512,256]{1,0:T(8,128)(2,1)S(1)}, u32[]{:S(2)}, u32[]{:S(2)}) collective-permute-start(bf16[512,256]{1,0:T(8,128)(2,1)} %get-tuple-element.39), channel_id=1, source_target_pairs={{0,8},{8,16},{16,24},{24,0},{1,9},{9,17},{17,25},{25,1},{2,10},{10... | collective-permute-start | bytes 786440 | tf_op jit(solution)/shard_map/ppermute | solution.py:19
  74.8 34.1 %collective-permute-start.15 = (bf16[512,256]{1,0:T(8,128)(2,1)}, bf16[512,256]{1,0:T(8,128)(2,1)}, u32[]{:S(2)}, u32[]{:S(2)}) collective-permute-start(bf16[512,256]{1,0:T(8,128)(2,1)} %get-tuple-element.40), channel_id=1, source_target_pairs={{0,24},{8,0},{16,8},{24,16},{1,25},{9,1},{17,9},{25,17},{2,26},{10... | collective-permute-start | bytes 786440 | tf_op jit(solution)/shard_map/ppermute | solution.py:19
  76.0 39.1 %collective-permute-start.14 = (bf16[512,256]{1,0:T(8,128)(2,1)S(1)}, bf16[512,256]{1,0:T(8,128)(2,1)}, u32[]{:S(2)}, u32[]{:S(2)}) collective-permute-start(bf16[512,256]{1,0:T(8,128)(2,1)S(1)} %get-tuple-element.41), channel_id=1, source_target_pairs={{0,16},{8,24},{16,0},{24,8},{1,17},{9,25},{17,1},{25,9},{2,18},{10... | collective-permute-start | bytes 786440 | tf_op jit(solution)/shard_map/ppermute | solution.py:19
  116.3 142.9 %collective-permute-start.16 = (bf16[512,128]{1,0:T(8,128)(2,1)S(1)}, bf16[512,128]{1,0:T(8,128)(2,1)S(1)}, u32[]{:S(2)}, u32[]{:S(2)}) collective-permute-start(bf16[512,128]{1,0:T(8,128)(2,1)S(1)} %constant_dynamic-slice_fusion), channel_id=1, source_target_pairs={{0,32},{32,0},{1,33},{33,1},{2,34},{34,2},{3,35},{35,3},{4,36},{36... | collective-permute-start | bytes 393224 | tf_op jit(solution)/shard_map/ppermute | solution.py:19
  126.7 135.6 %copy-start.1 = (f32[512,2048]{1,0:T(8,128)S(1)}, f32[512,2048]{1,0:T(8,128)}, u32[]{:S(2)}) copy-start(f32[512,2048]{1,0:T(8,128)} %copy-done) | copy-start | bytes 12582916
  264.4 13.4 %collective-permute-start.17 = (bf16[512,256]{0,1:T(8,128)(2,1)S(1)}, bf16[512,256]{0,1:T(8,128)(2,1)S(1)}, u32[]{:S(2)}, u32[]{:S(2)}) collective-permute-start(bf16[512,256]{0,1:T(8,128)(2,1)S(1)} %get-tuple-element.36), channel_id=1, source_target_pairs={{1,0},{2,1},{3,2},{5,4},{6,5},{7,6},{9,8},{10,9},{11,10},{13,12},{... | collective-permute-start | bytes 786440 | tf_op jit(solution)/shard_map/ppermute | solution.py:23
  266.9 31.4 %collective-permute-start.10 = (bf16[4,128,768]{2,1,0:T(8,128)(2,1)}, bf16[4,128,768]{2,1,0:T(8,128)(2,1)S(1)}, u32[]{:S(2)}, u32[]{:S(2)}) collective-permute-start(bf16[4,128,768]{2,1,0:T(8,128)(2,1)} %fusion.8), channel_id=1, source_target_pairs={{0,192},{64,0},{128,64},{192,128},{1,193},{65,1},{129,65},{193,129... | collective-permute-start | bytes 2359304 | tf_op jit(solution)/shard_map/ppermute | solution.py:19
  269.7 28.7 %collective-permute-start.11 = (bf16[4,128,768]{2,1,0:T(8,128)(2,1)}, bf16[4,128,768]{2,1,0:T(8,128)(2,1)}, u32[]{:S(2)}, u32[]{:S(2)}) collective-permute-start(bf16[4,128,768]{2,1,0:T(8,128)(2,1)} %fusion.8), channel_id=1, source_target_pairs={{0,128},{64,192},{128,0},{192,64},{1,129},{65,193},{129,1},{193,65... | collective-permute-start | bytes 2359304 | tf_op jit(solution)/shard_map/ppermute | solution.py:19
  270.0 37.8 %collective-permute-start.12 = (bf16[4,128,768]{2,1,0:T(8,128)(2,1)}, bf16[4,128,768]{2,1,0:T(8,128)(2,1)}, u32[]{:S(2)}, u32[]{:S(2)}) collective-permute-start(bf16[4,128,768]{2,1,0:T(8,128)(2,1)} %fusion.8), channel_id=1, source_target_pairs={{0,64},{64,128},{128,192},{192,0},{1,65},{65,129},{129,193},{193,1... | collective-permute-start | bytes 2359304 | tf_op jit(solution)/shard_map/ppermute | solution.py:19
  271.0 12.0 %collective-permute-start.19 = (bf16[512,256]{0,1:T(8,128)(2,1)S(1)}, bf16[512,256]{0,1:T(8,128)(2,1)S(1)}, u32[]{:S(2)}, u32[]{:S(2)}) collective-permute-start(bf16[512,256]{0,1:T(8,128)(2,1)S(1)} %get-tuple-element.37), channel_id=1, source_target_pairs={{3,0},{7,4},{11,8},{15,12},{19,16},{23,20},{27,24},{31,28},{35,32}... | collective-permute-start | bytes 786440 | tf_op jit(solution)/shard_map/ppermute | solution.py:23
  277.8 18.8 %collective-permute-start.18 = (bf16[512,256]{0,1:T(8,128)(2,1)S(1)}, bf16[512,256]{0,1:T(8,128)(2,1)S(1)}, u32[]{:S(2)}, u32[]{:S(2)}) collective-permute-start(bf16[512,256]{0,1:T(8,128)(2,1)S(1)} %get-tuple-element.38), channel_id=1, source_target_pairs={{2,0},{3,1},{6,4},{7,5},{10,8},{11,9},{14,12},{15,13},{18,16},{19,... | collective-permute-start | bytes 786440 | tf_op jit(solution)/shard_map/ppermute | solution.py:23
